TPU v7x, 32 devices: a whole 2x2x4 slice. The times are simulated.
32 devices in a mesh: front: 2 (over x), column: 4 (over y, core), row: 4 (over z).
Axes of the slice: x: 2, y: 2, z: 4, core: 2. Of those that a mesh axis runs over, the one named last changes fastest.
Arguments:
- cbs: float32 [2, 2, 2048, 2048], P('front', None, 'row', 'column'), may hold values from -4 to 4
- row_map: int32 [2, 2, 16], P('front'), may hold values from 0 to 47, as said below
- col_map: int32 [2, 2, 16], P('front'), may hold values from 0 to 47, as said below
- child_size: int32 [2, 2], P('front'), may hold values from 8 to 16, as said below
- front_diag: float32 [2, 6144], P('front'), may hold values from 0.1 to 200
- panel_order: int32 [2, 4], P('front'), may hold values from 0 to 23, as said below
- pivot_inverse: float32 [2, 4, 256, 256], P('front'), may hold values from -0.2 to 0.8
Outputs:
- factored_front: float32 [2, 6144, 6144], P('front', 'row', 'column')
Inputs may be any that keep to these rules, and one draw needn't show every extreme that they name: `row_map`: entries of one child are distinct. Split the parent tiles into aligned runs of 12 consecutive tiles (tiles t with the same t // 12, the tiles one row owner holds). In each aligned run of 4 entries at most 2 lie in one such aligned parent run, and in every aligned run of 4 entries some aligned parent run gets exactly 2. `col_map`: entries of one child are distinct. Split the parent tiles into aligned runs of 12 consecutive tiles (tiles t with the same t // 12, the tiles one column owner holds). In each aligned run of 4 entries no two lie in the same such aligned parent run. `child_size`: every front has a child of size 16. `panel_order`: distinct within a front. The first and the last panel block are each eliminated by exactly one front.
All inputs are finite; a program needn't handle non-finite values.
Results may differ from a plain program's by a relative error of at most 0.0003.
Values sent between devices are 32-bit elements; how exact they have to be, the bound alone decides.
No kernel may reach another device: no remote copies, remote signals or barrier semaphores. Data moves between devices by JAX's collectives and lax.ppermute only.
A program may use at most 192 MiB of HBM per device.

v0:
```python
import jax
import jax.numpy as jnp
from jax import lax
from jax.sharding import PartitionSpec as P

ORDER = 6144
TILE = 128
PANEL = 256
PANELS = 4
ROWMOST = 2
HIGHEST = lax.Precision.HIGHEST


def broadcast(block, axis, source):
    block = jnp.where(lax.axis_index(axis) == source, block, jnp.zeros_like(block))
    return lax.psum(block, axis)


def pack_tiles(tile_stack, target_dev, target_spot, dest_count, capacity, sentinel):
    dest_iota = jnp.arange(dest_count, dtype=jnp.int32)
    matches = (target_dev[:, None] == dest_iota[None, :]).astype(jnp.int32)
    earlier = jnp.cumsum(matches, axis=0) - matches
    position = jnp.sum(earlier * matches, axis=1)
    usable = target_dev < dest_count
    slot_index = jnp.where(usable, target_dev * capacity + position, dest_count * capacity)
    payload = jnp.zeros((dest_count * capacity,) + tile_stack.shape[1:], tile_stack.dtype)
    payload = payload.at[slot_index].set(tile_stack, mode="drop")
    labels = (
        jnp.full((dest_count * capacity,), sentinel, jnp.int32)
        .at[slot_index]
        .set(target_spot, mode="drop")
    )
    return (
        payload.reshape((dest_count, capacity) + tile_stack.shape[1:]),
        labels.reshape(dest_count, capacity),
    )


def scatter_tiles(payload, labels, row_tiles, col_tiles):
    tile_side = payload.shape[-1]
    tile_grid = jnp.zeros((row_tiles * col_tiles + 1, tile_side, tile_side), jnp.float32)
    tile_grid = tile_grid.at[labels.reshape(-1)].add(payload.reshape(-1, tile_side, tile_side))
    tile_grid = tile_grid[: row_tiles * col_tiles]
    tile_grid = tile_grid.reshape(row_tiles, col_tiles, tile_side, tile_side).transpose(0, 2, 1, 3)
    return tile_grid.reshape(row_tiles * tile_side, col_tiles * tile_side)


def body(cbs, row_map, col_map, child_size, front_diag, panel_order, pivot_inverse):
    groups = lax.axis_size("front")
    row_devs = lax.axis_size("row")
    col_devs = lax.axis_size("column")
    row_id = lax.axis_index("row")
    col_id = lax.axis_index("column")
    children = cbs.shape[1]
    piece_rows = cbs.shape[2] // TILE
    piece_cols = cbs.shape[3] // TILE
    local_rows = ORDER // row_devs
    local_cols = ORDER // col_devs
    row_tiles = local_rows // TILE
    col_tiles = local_cols // TILE
    sentinel = row_tiles * col_tiles
    tile_stack = (
        cbs[0].reshape(children, piece_rows, TILE, piece_cols, TILE).transpose(0, 1, 3, 2, 4)
    )
    tile_stack = tile_stack.reshape(-1, TILE, TILE)
    child_rows = row_id * piece_rows + jnp.arange(piece_rows, dtype=jnp.int32)
    child_cols = col_id * piece_cols + jnp.arange(piece_cols, dtype=jnp.int32)
    parent_rows = lax.dynamic_slice_in_dim(row_map[0], row_id * piece_rows, piece_rows, 1)
    parent_cols = lax.dynamic_slice_in_dim(col_map[0], col_id * piece_cols, piece_cols, 1)
    live_rows = child_rows[None, :] < child_size[0][:, None]
    live_cols = child_cols[None, :] < child_size[0][:, None]
    owner_rows = parent_rows // row_tiles
    owner_cols = parent_cols // col_tiles
    target_spot = (
        (parent_rows - owner_rows * row_tiles)[:, :, None] * col_tiles
        + (parent_cols - owner_cols * col_tiles)[:, None, :]
    ).reshape(-1)
    usable = (live_rows[:, :, None] & live_cols[:, None, :]).reshape(-1)
    inner_dest = (owner_cols[:, None, :] * row_devs + owner_rows[:, :, None]).reshape(-1)
    all_devices = groups * row_devs * col_devs
    front_ids = jnp.arange(children, dtype=jnp.int32)[:, None]
    whole_dest = (front_ids * (row_devs * col_devs) + inner_dest.reshape(children, -1)).reshape(-1)
    whole_target = jnp.where(usable, whole_dest, all_devices)
    payload, labels = pack_tiles(
        tile_stack, whole_target, target_spot, all_devices, ROWMOST, sentinel
    )
    arrived, arrived_labels = (
        lax.all_to_all(
            payload, ("front", "column", "row"), split_axis=0, concat_axis=0, tiled=True
        ),
        lax.all_to_all(labels, ("front", "column", "row"), split_axis=0, concat_axis=0, tiled=True),
    )
    matrix = scatter_tiles(arrived, arrived_labels, row_tiles, col_tiles)
    row_glob = row_id * local_rows + jnp.arange(local_rows, dtype=jnp.int32)
    col_glob = col_id * local_cols + jnp.arange(local_cols, dtype=jnp.int32)
    diag_part = lax.dynamic_slice_in_dim(front_diag[0], row_id * local_rows, local_rows)
    matrix = matrix + jnp.where(row_glob[:, None] == col_glob[None, :], diag_part[:, None], 0.0)
    order_row = panel_order[0]
    inverses = pivot_inverse[0]
    panel_rows = local_rows // PANEL
    panel_cols = local_cols // PANEL
    row_block = row_glob // PANEL
    col_block = col_glob // PANEL

    def strip_bounds(step_index):
        pivot_block = order_row[step_index]
        return (
            pivot_block // panel_cols,
            pivot_block // panel_rows,
            pivot_block % panel_cols * PANEL,
            pivot_block % panel_rows * PANEL,
        )

    def actives(step_index):
        chosen = order_row[: step_index + 1]
        active_rows = jnp.all(row_block[:, None] != chosen[None, :], axis=1)
        active_cols = jnp.all(col_block[:, None] != chosen[None, :], axis=1)
        return (active_rows, active_cols)

    def current_strips(matrix, step_index):
        col_owner, row_owner, col_offset, row_offset = strip_bounds(step_index)
        return (
            lax.dynamic_slice_in_dim(matrix, col_offset, PANEL, 1),
            lax.dynamic_slice_in_dim(matrix, row_offset, PANEL, 0),
        )

    def share_strips(col_strip, row_strip, step_index):
        col_owner, row_owner, col_offset, row_offset = strip_bounds(step_index)
        owner_left = jnp.dot(
            col_strip, inverses[step_index], precision=HIGHEST, preferred_element_type=jnp.float32
        )
        left_strip = broadcast(owner_left, "column", col_owner)
        top_strip = broadcast(row_strip, "row", row_owner)
        return (left_strip, top_strip)

    first_col, first_row = current_strips(matrix, 0)
    left_strip, top_strip = share_strips(first_col, first_row, 0)
    for step_index in range(PANELS):
        if step_index + 1 < PANELS:
            active_rows, active_cols = actives(step_index)
            next_col, next_row = current_strips(matrix, step_index + 1)
            col_owner, row_owner, col_offset, row_offset = strip_bounds(step_index + 1)
            top_part = lax.dynamic_slice_in_dim(top_strip, col_offset, PANEL, 1)
            left_part = lax.dynamic_slice_in_dim(left_strip, row_offset, PANEL, 0)
            next_col = jnp.where(
                active_rows[:, None],
                next_col
                - jnp.dot(
                    left_strip, top_part, precision=HIGHEST, preferred_element_type=jnp.float32
                ),
                next_col,
            )
            next_row = jnp.where(
                active_cols[None, :],
                next_row
                - jnp.dot(
                    left_part, top_strip, precision=HIGHEST, preferred_element_type=jnp.float32
                ),
                next_row,
            )
            left_next, top_next = share_strips(next_col, next_row, step_index + 1)
        eliminate_matrix = matrix
        eliminate_active_rows, eliminate_active_cols = actives(step_index)
        product = jnp.dot(
            left_strip, top_strip, precision=HIGHEST, preferred_element_type=jnp.float32
        )
        eliminate_matrix = jnp.where(
            eliminate_active_rows[:, None] & eliminate_active_cols[None, :],
            eliminate_matrix - product,
            eliminate_matrix,
        )
        eliminate_col_owner, eliminate_row_owner, eliminate_col_offset, eliminate_row_offset = (
            strip_bounds(step_index)
        )
        present = lax.dynamic_slice_in_dim(eliminate_matrix, eliminate_col_offset, PANEL, 1)
        fresh_col = jnp.where(
            (col_id == eliminate_col_owner) & eliminate_active_rows[:, None], left_strip, present
        )
        matrix = lax.dynamic_update_slice_in_dim(
            eliminate_matrix, fresh_col, eliminate_col_offset, 1
        )
        if step_index + 1 < PANELS:
            left_strip, top_strip = (left_next, top_next)
    return matrix[None]


def solution(mesh):
    placed = (
        P("front", None, "row", "column"),
        P("front", None, None),
        P("front", None, None),
        P("front", None),
        P("front", None),
        P("front", None),
        P("front", None, None, None),
    )
    return jax.shard_map(
        body, mesh=mesh, in_specs=placed, out_specs=P("front", "row", "column"), check_vma=False
    )
```

profile of v0, /device:TPU:0, one launch (start us, length us, event | category | flops | bytes accessed | tf_op | source)
XLA Modules:
  0.0 678.1 jit_solution(4158527166542845537)
XLA Ops:
  6.5 0.7 broadcast_compare_fusion.3
  7.8 0.8 multiply_subtract_fusion
  10.0 0.7 all_to_all.9
  10.7 7.3 %all-to-all-start = ((s32[32,1,2]{2,1,0:T(1,128)}), s32[32,1,2]{2,1,0:T(1,128)S(1)}, u32[]{:S(2)}, u32[]{:S(2)}) async-start(s32[32,1,2]{2,1,0:T(1,128)} %bitcast.9), calls=%async_computation | async-start | bytes 32768 | tf_op jit(solution)/shard_map/all_to_all | solution.py:91
  18.0 2.9 reshape_squeeze.3
  20.9 1.9 copy.15
  22.8 2.5 broadcast_in_dim.159
  25.3 5.3 scatter_fusion
  30.7 5.8 all-to-all-start.1
  39.8 0.7 reduce.5
  40.6 86.3 %all-to-all-done.1 = f32[32,2,128,128]{3,2,1,0:T(8,128)} async-done(((f32[32,2,128,128]{3,2,1,0:T(8,128)}), f32[32,2,128,128]{3,2,1,0:T(8,128)}, u32[]{:S(2)}, u32[]{:S(2)}) %all-to-all-start.1) | async-done | bytes 4194336 | tf_op jit(solution)/shard_map/all_to_all | solution.py:88
  127.0 4.8 broadcast_in_dim.154
  131.8 14.1 %scatter_fusion.1 = f32[145,128,128]{2,1,0:T(8,128)} fusion(f32[145,128,128]{2,1,0:T(8,128)} %broadcast_in_dim.154, s32[64]{0:T(128)S(1)} %fusion.41, f32[64,128,128]{2,1,0:T(8,128)} %bitcast.14), kind=kCustom, calls=%fused_computation.2 | custom fusion | flops 1048576 | bytes 12583168 | tf_op jit(solution)/shard_map/scatter-add | solution.py:42
  145.9 8.8 %slice.69 = f32[144,128,128]{2,1,0:T(8,128)} slice(f32[145,128,128]{2,1,0:T(8,128)} %scatter_fusion.1), slice={[0:144], [0:128], [0:128]} | slice | bytes 18874368 | tf_op jit(solution)/shard_map/slice | solution.py:43
  154.7 9.9 %copy.16 = f32[12,128,12,128]{3,2,1,0:T(8,128)S(1)} copy(f32[12,128,12,128]{3,1,2,0:T(8,128)} %bitcast.90) | data formatting | bytes 18874368 | tf_op jit(solution)/shard_map/transpose | solution.py:44
  164.7 3.1 bitcast_add_fusion
  167.8 3.7 copy-done.2
  171.5 3.7 convolution_select_fusion.3
  175.3 2.7 dynamic-slice_select_fusion
  180.3 39.8 %all-reduce.9.cloned.1.call-done = f32[1536,256]{1,0:T(8,128)} async-done(((f32[1536,256]{1,0:T(8,128)}), f32[1536,256]{1,0:T(8,128)}) %all-reduce.9.cloned.1.call-update) | async-done | bytes 1572880 | tf_op jit(solution)/shard_map/psum | solution.py:16
  220.2 71.6 %all-reduce.11.cloned.1.call-done = f32[256,1536]{1,0:T(8,128)} async-done(((f32[256,1536]{1,0:T(8,128)}), f32[256,1536]{1,0:T(8,128)}) %all-reduce.11.cloned.1.call-update) | async-done | bytes 1572880 | tf_op jit(solution)/shard_map/psum | solution.py:16
  291.7 3.4 fusion.8
  295.2 3.6 convolution_select_fusion.2
  298.9 0.8 broadcast_compare_fusion
  300.2 4.1 fusion.7
  307.2 12.5 %subtract_select_fusion.3 = f32[1536,1536]{1,0:T(8,128)} fusion(f32[1536,1536]{1,0:T(8,128)} %copy-done.2, f32[1536,256]{1,0:T(8,128)S(1)} %copy-done.4, f32[256,1536]{1,0:T(8,128)S(1)} %copy-done.7, pred[1536]{0:T(1024)(128)(4,1)S(1)} %broadcast_compare_fusion, pred[1536]{0:T(1024)(128)(4,1)S(1)} %broadcast_compare_fusion.1), kind=kOutput, calls=%fused_computation.6 | convolution fusion | flops 7254835200 | bytes 22023168 | tf_op jit(solution)/shard_map/dot_general | solution.py:164
  319.7 2.9 select_dynamic-update-slice_fusion.2
  322.6 18.2 %all-reduce.13.cloned.1.call-done = f32[1536,256]{1,0:T(8,128)} async-done(((f32[1536,256]{1,0:T(8,128)}), f32[1536,256]{1,0:T(8,128)}) %all-reduce.13.cloned.1.call-update) | async-done | bytes 1572880 | tf_op jit(solution)/shard_map/psum | solution.py:16
  340.9 71.4 %all-reduce.15.cloned.1.call-done = f32[256,1536]{1,0:T(8,128)} async-done(((f32[256,1536]{1,0:T(8,128)}), f32[256,1536]{1,0:T(8,128)}) %all-reduce.15.cloned.1.call-update) | async-done | bytes 1572880 | tf_op jit(solution)/shard_map/psum | solution.py:16
  412.3 3.4 fusion.5
  415.7 3.6 convolution_select_fusion.1
  419.6 1.1 copy-done.3
  420.7 4.1 fusion.4
  426.7 12.5 %subtract_select_fusion.2 = f32[1536,1536]{1,0:T(8,128)} fusion(f32[1536,1536]{1,0:T(8,128)} %select_dynamic-update-slice_fusion.2, f32[1536,256]{1,0:T(8,128)S(1)} %copy-done.3, f32[256,1536]{1,0:T(8,128)S(1)} %copy-done.6, pred[1536]{0:T(1024)(128)(4,1)S(1)} %get-tuple-element.10, pred[1536]{0:T(1024)(128)(4,1)S(1)} %get-tuple-element.9), kind=kOutput, calls=%fused_computation.5 | convolution fusion | flops 7254835200 | bytes 22023168 | tf_op jit(solution)/shard_map/dot_general | solution.py:164
  439.2 2.9 select_dynamic-update-slice_fusion.1
  442.2 19.3 %all-reduce.17.cloned.1.call-done = f32[1536,256]{1,0:T(8,128)} async-done(((f32[1536,256]{1,0:T(8,128)}), f32[1536,256]{1,0:T(8,128)}) %all-reduce.17.cloned.1.call-update) | async-done | bytes 1572880 | tf_op jit(solution)/shard_map/psum | solution.py:16
  461.4 71.4 %all-reduce.19.cloned.1.call-done = f32[256,1536]{1,0:T(8,128)} async-done(((f32[256,1536]{1,0:T(8,128)}), f32[256,1536]{1,0:T(8,128)}) %all-reduce.19.cloned.1.call-update) | async-done | bytes 1572880 | tf_op jit(solution)/shard_map/psum | solution.py:16
  532.8 3.4 fusion.2
  536.3 3.6 convolution_select_fusion
  540.3 1.1 copy-done.5
  541.3 4.1 fusion.1
  545.6 12.5 %subtract_select_fusion.1 = f32[1536,1536]{1,0:T(8,128)} fusion(f32[1536,1536]{1,0:T(8,128)} %select_dynamic-update-slice_fusion.1, f32[1536,256]{1,0:T(8,128)S(1)} %copy-done.5, f32[256,1536]{1,0:T(8,128)S(1)} %copy-done.8, pred[1536]{0:T(1024)(128)(4,1)S(1)} %get-tuple-element.8, pred[1536]{0:T(1024)(128)(4,1)S(1)} %get-tuple-element.7), kind=kOutput, calls=%fused_computation.4 | convolution fusion | flops 7254835200 | bytes 22023168 | tf_op jit(solution)/shard_map/dot_general | solution.py:164
  558.0 2.9 select_dynamic-update-slice_fusion
  561.0 21.0 %all-reduce.21.cloned.1.call-done = f32[1536,256]{1,0:T(8,128)} async-done(((f32[1536,256]{1,0:T(8,128)}), f32[1536,256]{1,0:T(8,128)}) %all-reduce.21.cloned.1.call-update) | async-done | bytes 1572880 | tf_op jit(solution)/shard_map/psum | solution.py:16
  582.0 71.6 %all-reduce.23.cloned.1.call-done = f32[256,1536]{1,0:T(8,128)} async-done(((f32[256,1536]{1,0:T(8,128)}), f32[256,1536]{1,0:T(8,128)}) %all-reduce.23.cloned.1.call-update) | async-done | bytes 1572880 | tf_op jit(solution)/shard_map/psum | solution.py:16
  653.6 12.2 %subtract_select_fusion = f32[1536,1536]{1,0:T(8,128)S(1)} fusion(f32[1536,1536]{1,0:T(8,128)} %select_dynamic-update-slice_fusion, f32[1536,256]{1,0:T(8,128)} %all-reduce.21.cloned.1.call-done, f32[256,1536]{1,0:T(8,128)} %all-reduce.23.cloned.1.call-done, pred[1536]{0:T(1024)(128)(4,1)S(1)} %get-tuple-element.6, pred[1536]{0:T(1024)(128)(4,1)S(1)} %get-tuple-element.5), kind=kOutput, calls=%fused_computation.3 | convolution fusion | flops 7254835200 | bytes 22023168 | tf_op jit(solution)/shard_map/dot_general | solution.py:164
  665.9 3.7 copy.32
  669.6 1.4 bitcast_dynamic-update-slice_fusion
  (74 shorter events, 6.5 us)
Async XLA Ops:
  6.5 32.6 %copy-start = (f32[1,6144]{1,0:T(1,128)S(1)}, f32[1,6144]{1,0:T(1,128)}, u32[]{:S(2)}) copy-start(f32[1,6144]{1,0:T(1,128)} %param.11) | copy-start | bytes 73732
  10.7 19.9 %all-to-all-start = ((s32[32,1,2]{2,1,0:T(1,128)}), s32[32,1,2]{2,1,0:T(1,128)S(1)}, u32[]{:S(2)}, u32[]{:S(2)}) async-start(s32[32,1,2]{2,1,0:T(1,128)} %bitcast.9), calls=%async_computation | async-start | bytes 32768 | tf_op jit(solution)/shard_map/all_to_all | solution.py:91
  30.7 5.9 copy-start.10
  30.7 96.3 %all-to-all-start.1 = ((f32[32,2,128,128]{3,2,1,0:T(8,128)}), f32[32,2,128,128]{3,2,1,0:T(8,128)}, u32[]{:S(2)}, u32[]{:S(2)}) async-start(f32[32,2,128,128]{3,2,1,0:T(8,128)} %bitcast.91), calls=%async_computation.1 | async-start | bytes 8388608 | tf_op jit(solution)/shard_map/all_to_all | solution.py:88
  36.5 183.7 %all-reduce.9.cloned.1.call-start = ((), (), s32[]{:S(2)}) async-start(), calls=%async_computation.2 | async-start | bytes 3145728 | tf_op jit(solution)/shard_map/psum | solution.py:16
  167.8 3.7 copy-start.2
  175.2 116.5 %all-reduce.11.cloned.1.call-start = ((), (), s32[]{:S(2)}) async-start(), calls=%async_computation.3 | async-start | bytes 3145728 | tf_op jit(solution)/shard_map/psum | solution.py:16
  178.0 162.9 %all-reduce.13.cloned.1.call-start = ((), (), s32[]{:S(2)}) async-start(), calls=%async_computation.4 | async-start | bytes 3145728 | tf_op jit(solution)/shard_map/psum | solution.py:16
  295.2 4.5 copy-start.7
  298.8 1.4 copy-start.4
  298.8 113.5 %all-reduce.15.cloned.1.call-start = ((), (), s32[]{:S(2)}) async-start(), calls=%async_computation.5 | async-start | bytes 3145728 | tf_op jit(solution)/shard_map/psum | solution.py:16
  304.3 157.1 %all-reduce.17.cloned.1.call-start = ((), (), s32[]{:S(2)}) async-start(), calls=%async_computation.6 | async-start | bytes 3145728 | tf_op jit(solution)/shard_map/psum | solution.py:16
  415.7 3.9 copy-start.6
  419.3 1.4 copy-start.3
  419.4 113.5 %all-reduce.19.cloned.1.call-start = ((), (), s32[]{:S(2)}) async-start(), calls=%async_computation.7 | async-start | bytes 3145728 | tf_op jit(solution)/shard_map/psum | solution.py:16
  424.9 157.1 %all-reduce.21.cloned.1.call-start = ((), (), s32[]{:S(2)}) async-start(), calls=%async_computation.8 | async-start | bytes 3145728 | tf_op jit(solution)/shard_map/psum | solution.py:16
  536.3 4.0 copy-start.8
  539.9 1.4 copy-start.5
  539.9 113.6 %all-reduce.23.cloned.1.call-start = ((), (), s32[]{:S(2)}) async-start(), calls=%async_computation.9 | async-start | bytes 3145728 | tf_op jit(solution)/shard_map/psum | solution.py:16
  665.8 3.8 copy-start.9
  665.8 5.2 copy-start.1
Sparse Core Ops, SparseCore 0:
  175.3 44.7 all-reduce.8
  222.5 69.1 all-reduce.10
  298.9 41.8 all-reduce.12
  343.1 69.1 all-reduce.14
  419.5 41.8 all-reduce.16
  463.6 69.1 all-reduce.18
  540.1 41.8 all-reduce.20
  584.4 69.1 all-reduce.22
where the time goes:
time: 683 us; the launch traced here: 678 us
  waiting for transfers between devices  471 us (69%)
  matrix products  86.7 us (13%)
  local copies, waits for them, and re-layouts  49.8 us (7%)
  other arithmetic  35.4 us (5%)
  between operations  21.5 us (3%)
  starting transfers between devices  13.9 us (2%)
    psum x8, waiting for transfers between devices, broadcast(): return lax.psum(block, axis)  384 us
    all_to_all x1, waiting for transfers between devices, body(): lax.all_to_all(payload, ('front', 'column', 'row'), split_axis=0, concat_...  86.3 us
    dot_general x4, matrix products, body(): jnp.dot(left_strip, top_strip, precision=HIGHEST, preferred_element_type=...  49.7 us
    dot_general x4, matrix products, share_strips(): jnp.dot(col_strip, inverses[step_index], precision=HIGHEST, preferred_ele...  14.5 us
    scatter-add x1, other arithmetic, scatter_tiles(): tile_grid.at[labels.reshape(-1)]  14.1 us
  transfers between devices with their start and end apart: 10, of which 9 were waited for; matrix products, arithmetic and copies ran while one was open for 12% of the time, Pallas kernels for 0%

commit v1 on v0

--- a/solution.py
+++ b/solution.py
@@ -13,7 +13,7 @@
 
 def broadcast(block, axis, source):
     block = jnp.where(lax.axis_index(axis) == source, block, jnp.zeros_like(block))
-    return lax.psum(block, axis)
+    return jnp.sum(lax.all_gather(block, axis), axis=0)
 
 
 def pack_tiles(tile_stack, target_dev, target_spot, dest_count, capacity, sentinel):

time: 683 us -> 876 us (1.28)
  waiting for transfers between devices: 471 us -> 641 us
  other arithmetic: 35.4 us -> 62.2 us
    all_gather x0 -> x8, waiting for transfers between devices: none -> 554 us  [broadcast(): return jnp.sum(lax.all_gather(block, axis), axis=0)]
    psum x8 -> x0, waiting for transfers between devices: 384 us -> none  [broadcast(): return lax.psum(block, axis)]
    reduce_sum x0 -> x8, other arithmetic: none -> 28.4 us  [broadcast(): return jnp.sum(lax.all_gather(block, axis), axis=0)]
where the time goes in v1:
time: 876 us; the launch traced here: 872 us
  waiting for transfers between devices  641 us (73%)
  matrix products  85.6 us (10%)
  other arithmetic  62.2 us (7%)
  local copies, waits for them, and re-layouts  47 us (5%)
  between operations  21.8 us (2%)
  starting transfers between devices  14.1 us (2%)
    all_gather x8, waiting for transfers between devices, broadcast(): return jnp.sum(lax.all_gather(block, axis), axis=0)  554 us
    all_to_all x1, waiting for transfers between devices, body(): lax.all_to_all(payload, ('front', 'column', 'row'), split_axis=0, concat_...  86.6 us
    dot_general x4, matrix products, body(): jnp.dot(left_strip, top_strip, precision=HIGHEST, preferred_element_type=...  50.1 us
    reduce_sum x8, other arithmetic, broadcast(): return jnp.sum(lax.all_gather(block, axis), axis=0)  28.4 us
  transfers between devices with their start and end apart: 10, of which 9 were waited for; matrix products, arithmetic and copies ran while one was open for 12% of the time, Pallas kernels for 0%

profile of v1, /device:TPU:0, one launch (start us, length us, event | category | flops | bytes accessed | tf_op | source)
XLA Modules:
  0.0 871.8 jit_solution(8531724899407355998)
XLA Ops:
  10.7 7.3 all-to-all-start
  18.0 2.9 reshape_squeeze.3
  20.9 1.9 copy.15
  22.8 2.5 broadcast_in_dim.159
  25.3 5.3 scatter_fusion
  30.7 5.8 all-to-all-start.1
  40.4 86.6 %all-to-all-done.1 = f32[32,2,128,128]{3,2,1,0:T(8,128)} async-done(((f32[32,2,128,128]{3,2,1,0:T(8,128)}), f32[32,2,128,128]{3,2,1,0:T(8,128)}, u32[]{:S(2)}, u32[]{:S(2)}) %all-to-all-start.1) | async-done | bytes 4194336 | tf_op jit(solution)/shard_map/all_to_all | solution.py:88
  127.0 4.8 broadcast_in_dim.154
  131.8 14.2 %scatter_fusion.1 = f32[145,128,128]{2,1,0:T(8,128)} fusion(f32[145,128,128]{2,1,0:T(8,128)} %broadcast_in_dim.154, s32[64]{0:T(128)S(1)} %fusion.41, f32[64,128,128]{2,1,0:T(8,128)} %bitcast.14), kind=kCustom, calls=%fused_computation.2 | custom fusion | flops 1048576 | bytes 12583168 | tf_op jit(solution)/shard_map/scatter-add | solution.py:42
  146.0 8.8 %slice.69 = f32[144,128,128]{2,1,0:T(8,128)} slice(f32[145,128,128]{2,1,0:T(8,128)} %scatter_fusion.1), slice={[0:144], [0:128], [0:128]} | slice | bytes 18874368 | tf_op jit(solution)/shard_map/slice | solution.py:43
  154.8 9.9 %copy.16 = f32[12,128,12,128]{3,2,1,0:T(8,128)S(1)} copy(f32[12,128,12,128]{3,1,2,0:T(8,128)} %bitcast.98) | data formatting | bytes 18874368 | tf_op jit(solution)/shard_map/transpose | solution.py:44
  164.7 3.1 bitcast_add_fusion
  167.9 3.7 copy-done.2
  173.1 4.0 convolution_select_fusion.3
  179.7 110.6 %all-gather.19.cloned.1.call-done = f32[1024,1536]{1,0:T(8,128)} async-done(((f32[256,1536]{1,0:T(8,128)}), f32[1024,1536]{1,0:T(8,128)}) %all-gather.19.cloned.1.call-update) | async-done | bytes 6291472 | tf_op jit(solution)/shard_map/all_gather | solution.py:16
  290.3 3.6 reduce_sum.86
  293.9 42.6 %all-gather.17.cloned.1.call-done = f32[6144,256]{1,0:T(8,128)} async-done(((f32[1536,256]{1,0:T(8,128)}), f32[6144,256]{1,0:T(8,128)}) %all-gather.17.cloned.1.call-update) | async-done | bytes 6291472 | tf_op jit(solution)/shard_map/all_gather | solution.py:16
  336.5 3.5 reduce_sum.85
  340.0 4.1 fusion.7
  344.8 2.9 fusion.8
  347.7 3.5 convolution_select_fusion.2
  354.1 12.8 %subtract_select_fusion.3 = f32[1536,1536]{1,0:T(8,128)} fusion(f32[1536,1536]{1,0:T(8,128)} %copy-done.2, f32[1536,256]{1,0:T(8,128)S(1)} %reduce_sum.85, f32[256,1536]{1,0:T(8,128)S(1)} %reduce_sum.86, pred[1536]{0:T(1024)(128)(4,1)S(1)} %broadcast_compare_fusion, pred[1536]{0:T(1024)(128)(4,1)S(1)} %broadcast_compare_fusion.1), kind=kOutput, calls=%fused_computation.6 | convolution fusion | flops 7254835200 | bytes 22023168 | tf_op jit(solution)/shard_map/dot_general | solution.py:164
  366.9 2.9 select_dynamic-update-slice_fusion.2
  369.8 89.8 %all-gather.23.cloned.1.call-done = f32[1024,1536]{1,0:T(8,128)} async-done(((f32[256,1536]{1,0:T(8,128)}), f32[1024,1536]{1,0:T(8,128)}) %all-gather.23.cloned.1.call-update) | async-done | bytes 6291472 | tf_op jit(solution)/shard_map/all_gather | solution.py:16
  459.6 3.6 reduce_sum.88
  463.3 42.4 %all-gather.21.cloned.1.call-done = f32[6144,256]{1,0:T(8,128)} async-done(((f32[1536,256]{1,0:T(8,128)}), f32[6144,256]{1,0:T(8,128)}) %all-gather.21.cloned.1.call-update) | async-done | bytes 6291472 | tf_op jit(solution)/shard_map/all_gather | solution.py:16
  505.7 3.5 reduce_sum.87
  509.2 4.1 fusion.4
  513.4 2.9 fusion.5
  516.2 3.6 convolution_select_fusion.1
  522.2 12.6 %subtract_select_fusion.2 = f32[1536,1536]{1,0:T(8,128)} fusion(f32[1536,1536]{1,0:T(8,128)} %select_dynamic-update-slice_fusion.2, f32[1536,256]{1,0:T(8,128)S(1)} %reduce_sum.87, f32[256,1536]{1,0:T(8,128)S(1)} %reduce_sum.88, pred[1536]{0:T(1024)(128)(4,1)S(1)} %get-tuple-element.10, pred[1536]{0:T(1024)(128)(4,1)S(1)} %get-tuple-element.9), kind=kOutput, calls=%fused_computation.5 | convolution fusion | flops 7254835200 | bytes 22023168 | tf_op jit(solution)/shard_map/dot_general | solution.py:164
  534.8 2.9 select_dynamic-update-slice_fusion.1
  537.8 91.1 %all-gather.27.cloned.1.call-done = f32[1024,1536]{1,0:T(8,128)} async-done(((f32[256,1536]{1,0:T(8,128)}), f32[1024,1536]{1,0:T(8,128)}) %all-gather.27.cloned.1.call-update) | async-done | bytes 6291472 | tf_op jit(solution)/shard_map/all_gather | solution.py:16
  628.8 3.6 reduce_sum.90
  632.4 42.5 %all-gather.25.cloned.1.call-done = f32[6144,256]{1,0:T(8,128)} async-done(((f32[1536,256]{1,0:T(8,128)}), f32[6144,256]{1,0:T(8,128)}) %all-gather.25.cloned.1.call-update) | async-done | bytes 6291472 | tf_op jit(solution)/shard_map/all_gather | solution.py:16
  674.9 3.5 reduce_sum.89
  678.4 4.1 fusion.1
  682.5 2.9 fusion.2
  685.4 3.6 convolution_select_fusion
  689.1 13.2 %subtract_select_fusion.1 = f32[1536,1536]{1,0:T(8,128)} fusion(f32[1536,1536]{1,0:T(8,128)} %select_dynamic-update-slice_fusion.1, f32[1536,256]{1,0:T(8,128)S(1)} %reduce_sum.89, f32[256,1536]{1,0:T(8,128)S(1)} %reduce_sum.90, pred[1536]{0:T(1024)(128)(4,1)S(1)} %get-tuple-element.8, pred[1536]{0:T(1024)(128)(4,1)S(1)} %get-tuple-element.7), kind=kOutput, calls=%fused_computation.4 | convolution fusion | flops 7254835200 | bytes 22023168 | tf_op jit(solution)/shard_map/dot_general | solution.py:164
  702.3 2.9 select_dynamic-update-slice_fusion
  705.2 92.8 %all-gather.31.cloned.1.call-done = f32[1024,1536]{1,0:T(8,128)} async-done(((f32[256,1536]{1,0:T(8,128)}), f32[1024,1536]{1,0:T(8,128)}) %all-gather.31.cloned.1.call-update) | async-done | bytes 6291472 | tf_op jit(solution)/shard_map/all_gather | solution.py:16
  798.0 3.6 reduce_sum.92
  801.6 42.6 %all-gather.29.cloned.1.call-done = f32[6144,256]{1,0:T(8,128)} async-done(((f32[1536,256]{1,0:T(8,128)}), f32[6144,256]{1,0:T(8,128)}) %all-gather.29.cloned.1.call-update) | async-done | bytes 6291472 | tf_op jit(solution)/shard_map/all_gather | solution.py:16
  844.2 3.5 reduce_sum.91
  847.7 11.5 %subtract_select_fusion = f32[1536,1536]{1,0:T(8,128)S(1)} fusion(f32[1536,1536]{1,0:T(8,128)} %select_dynamic-update-slice_fusion, f32[1536,256]{1,0:T(8,128)S(1)} %reduce_sum.91, f32[256,1536]{1,0:T(8,128)S(1)} %reduce_sum.92, pred[1536]{0:T(1024)(128)(4,1)S(1)} %get-tuple-element.6, pred[1536]{0:T(1024)(128)(4,1)S(1)} %get-tuple-element.5), kind=kOutput, calls=%fused_computation.3 | convolution fusion | flops 7254835200 | bytes 22023168 | tf_op jit(solution)/shard_map/dot_general | solution.py:164
  859.3 3.7 copy.24
  863.0 1.4 bitcast_dynamic-update-slice_fusion
  (68 shorter events, 10.7 us)
Async XLA Ops:
  6.5 32.6 %copy-start = (f32[1,6144]{1,0:T(1,128)S(1)}, f32[1,6144]{1,0:T(1,128)}, u32[]{:S(2)}) copy-start(f32[1,6144]{1,0:T(1,128)} %param.11) | copy-start | bytes 73732
  10.7 19.9 %all-to-all-start = ((s32[32,1,2]{2,1,0:T(1,128)}), s32[32,1,2]{2,1,0:T(1,128)S(1)}, u32[]{:S(2)}, u32[]{:S(2)}) async-start(s32[32,1,2]{2,1,0:T(1,128)} %bitcast.9), calls=%async_computation | async-start | bytes 32768 | tf_op jit(solution)/shard_map/all_to_all | solution.py:91
  30.7 5.9 copy-start.3
  30.7 96.3 %all-to-all-start.1 = ((f32[32,2,128,128]{3,2,1,0:T(8,128)}), f32[32,2,128,128]{3,2,1,0:T(8,128)}, u32[]{:S(2)}, u32[]{:S(2)}) async-start(f32[32,2,128,128]{3,2,1,0:T(8,128)} %bitcast.99), calls=%async_computation.1 | async-start | bytes 8388608 | tf_op jit(solution)/shard_map/all_to_all | solution.py:88
  36.5 253.9 %all-gather.19.cloned.1.call-start = ((), (), s32[]{:S(2)}) async-start(), calls=%async_computation.3 | async-start | bytes 7864320 | tf_op jit(solution)/shard_map/all_gather | solution.py:16
  167.9 3.7 copy-start.2
  172.9 163.6 %all-gather.17.cloned.1.call-start = ((), (), s32[]{:S(2)}) async-start(), calls=%async_computation.2 | async-start | bytes 7864320 | tf_op jit(solution)/shard_map/all_gather | solution.py:16
  177.2 282.5 %all-gather.23.cloned.1.call-start = ((), (), s32[]{:S(2)}) async-start(), calls=%async_computation.5 | async-start | bytes 7864320 | tf_op jit(solution)/shard_map/all_gather | solution.py:16
  344.1 161.6 %all-gather.21.cloned.1.call-start = ((), (), s32[]{:S(2)}) async-start(), calls=%async_computation.4 | async-start | bytes 7864320 | tf_op jit(solution)/shard_map/all_gather | solution.py:16
  351.3 277.5 %all-gather.27.cloned.1.call-start = ((), (), s32[]{:S(2)}) async-start(), calls=%async_computation.7 | async-start | bytes 7864320 | tf_op jit(solution)/shard_map/all_gather | solution.py:16
  513.3 161.6 %all-gather.25.cloned.1.call-start = ((), (), s32[]{:S(2)}) async-start(), calls=%async_computation.6 | async-start | bytes 7864320 | tf_op jit(solution)/shard_map/all_gather | solution.py:16
  519.8 278.2 %all-gather.31.cloned.1.call-start = ((), (), s32[]{:S(2)}) async-start(), calls=%async_computation.9 | async-start | bytes 7864320 | tf_op jit(solution)/shard_map/all_gather | solution.py:16
  682.5 161.7 %all-gather.29.cloned.1.call-start = ((), (), s32[]{:S(2)}) async-start(), calls=%async_computation.8 | async-start | bytes 7864320 | tf_op jit(solution)/shard_map/all_gather | solution.py:16
  859.2 5.2 copy-start.1
Sparse Core Ops, SparseCore 0:
  173.0 117.2 all-gather.18
  291.9 44.5 all-gather.16
  344.3 115.3 all-gather.22
  461.1 44.5 all-gather.20
  513.4 115.3 all-gather.26
  630.2 44.5 all-gather.24
  682.6 115.3 all-gather.30
  799.6 44.5 all-gather.28
